TPU v7x, 32 devices: a whole 2x2x4 slice. The times are simulated.
32 devices in a mesh: dp: 16 (over z, x, core), tensor: 2 (over y).
Axes of the slice: x: 2, y: 2, z: 4, core: 2. Of those that a mesh axis runs over, the one named last changes fastest.
Arguments:
- context: bfloat16 [4096, 4096], P('dp', 'tensor'), may hold values from -6 to 6
- w_out: bfloat16 [4096, 4096], P('tensor'), may hold values from -1 to 1
- teacher_input: bfloat16 [4096, 4096], P(('dp', 'tensor')), may hold values from -6 to 6
- teacher_gain: bfloat16 [4096], replicated, may hold values from 0.5 to 1.5
- layer_weights: float32 [2], replicated, may hold values from 0.3 to 1.5
- teacher_head: bfloat16 [4096, 4], replicated, may hold values from -16 to 16
- student_hidden: bfloat16 [4096, 3072], P(('dp', 'tensor')), may hold values from -6 to 6
- student_input: bfloat16 [4096, 768], P(('dp', 'tensor')), may hold values from -10 to 10
- down_weight: bfloat16 [3072, 768], P(('dp', 'tensor')), may hold values from -0.109375 to 0.109375
- student_gain: bfloat16 [768], replicated, may hold values from 0.5 to 1.5
- student_head: bfloat16 [768, 4], replicated, may hold values from -32 to 32
- labels: int32 [4096], P(('dp', 'tensor')), may hold values from 0 to 3
- lengths: int32 [8], replicated, may hold values from 64 to 512
Outputs:
- grad_down: float32 [3072, 768], P(('dp', 'tensor'))
- grad_head: float32 [768, 4], replicated
- loss: float32 [], replicated
All inputs are finite; a program needn't handle non-finite values.
Results may differ from a plain program's by a relative error of at most 0.0075.
Values may be sent and summed in bfloat16 or wider, within the bound.
No kernel may reach another device: no remote copies, remote signals or barrier semaphores. Data moves between devices by JAX's collectives and lax.ppermute only.
A program may use at most 128 MiB of HBM per device.

v0:
```python
import jax
import jax.numpy as jnp
from jax import lax
from jax.sharding import PartitionSpec as P

SEQ = 512
label_weight = 0.5
teacher_eps = 1e-05
student_eps = 1e-07


def norm_rows(values, gain_vec, epsilon):
    center = values - jnp.mean(values, axis=-1, keepdims=True)
    spread = jnp.mean(center * center, axis=-1, keepdims=True)
    inverse = lax.rsqrt(spread + epsilon)
    scaled = center * inverse
    return (scaled * gain_vec, scaled, inverse)


def folder(ordered, row_piece):
    return jnp.dot(ordered, row_piece, preferred_element_type=jnp.float32)


def local(
    context,
    w_out,
    teacher_input,
    teacher_gain,
    layer_weights,
    teacher_head,
    student_hidden,
    student_input,
    down_weight,
    student_gain,
    student_head,
    labels,
    lengths,
):
    tok_rows = teacher_input.shape[0]
    tensor_size = lax.axis_size("tensor")
    attention = lax.psum_scatter(
        jnp.dot(context, w_out, preferred_element_type=jnp.float32).astype(jnp.bfloat16),
        "tensor",
        scatter_dimension=0,
        tiled=True,
    ).astype(jnp.float32)
    residual = teacher_input.astype(jnp.float32)
    layer_out = norm_rows(residual + attention, teacher_gain.astype(jnp.float32), teacher_eps)[0]
    blended = (layer_weights[0] * residual + layer_weights[1] * layer_out).astype(jnp.bfloat16)
    teacher_logits = jnp.dot(blended, teacher_head, preferred_element_type=jnp.float32)
    teacher_logp = jax.nn.log_softmax(teacher_logits, axis=-1)
    teacher_prob = jnp.exp(teacher_logp)
    ffn_out = folder(
        student_hidden, lax.all_gather(down_weight, ("dp", "tensor"), axis=0, tiled=True)
    )
    student_scale = student_gain.astype(jnp.float32)
    normed, scaled, inverse = norm_rows(
        student_input.astype(jnp.float32) + ffn_out, student_scale, student_eps
    )
    features = normed.astype(jnp.bfloat16)
    student_logits = jnp.dot(features, student_head, preferred_element_type=jnp.float32)
    student_logp = jax.nn.log_softmax(student_logits, axis=-1)
    student_prob = jnp.exp(student_logp)
    first_token = (lax.axis_index("dp") * tensor_size + lax.axis_index("tensor")) * tok_rows
    positions = first_token + jnp.arange(tok_rows, dtype=jnp.int32)
    sentence = positions // SEQ
    matches = sentence[:, None] == jnp.arange(lengths.shape[0], dtype=jnp.int32)[None, :]
    lengths_tok = jnp.sum(jnp.where(matches, lengths[None, :], 0), axis=1)
    validity = (positions % SEQ < lengths_tok).astype(jnp.float32)
    onehot = (
        labels[:, None] == jnp.arange(teacher_logits.shape[1], dtype=jnp.int32)[None, :]
    ).astype(jnp.float32)
    token_loss = jnp.sum(
        teacher_prob * (teacher_logp - student_logp), axis=1
    ) - label_weight * jnp.sum(onehot * student_logp, axis=1)
    loss_part = jnp.sum(validity * token_loss)
    logit_grad = (
        validity[:, None]
        * ((1.0 + label_weight) * student_prob - teacher_prob - label_weight * onehot)
    ).astype(jnp.bfloat16)
    head_term = lax.dot_general(
        features, logit_grad, (((0,), (0,)), ((), ())), preferred_element_type=jnp.float32
    )
    norm_grad = (
        jnp.dot(logit_grad, student_head.T, preferred_element_type=jnp.float32) * student_scale
    )
    grad_out = (
        (
            norm_grad
            - jnp.mean(norm_grad, axis=-1, keepdims=True)
            - scaled * jnp.mean(norm_grad * scaled, axis=-1, keepdims=True)
        )
        * inverse
    ).astype(jnp.bfloat16)
    grad_down = lax.psum_scatter(
        lax.dot_general(
            student_hidden, grad_out, (((0,), (0,)), ((), ())), preferred_element_type=jnp.float32
        ),
        ("dp", "tensor"),
        scatter_dimension=0,
        tiled=True,
    )
    head_total, loss_total, count_total = lax.psum(
        (head_term, loss_part, jnp.sum(validity)), ("dp", "tensor")
    )
    return (grad_down, head_total, loss_total / count_total)


def solution(mesh):
    return jax.shard_map(
        local,
        mesh=mesh,
        in_specs=(
            P("dp", "tensor"),
            P("tensor", None),
            P(("dp", "tensor"), None),
            P(),
            P(),
            P(),
            P(("dp", "tensor"), None),
            P(("dp", "tensor"), None),
            P(("dp", "tensor"), None),
            P(),
            P(),
            P(("dp", "tensor")),
            P(),
        ),
        out_specs=(P(("dp", "tensor"), None), P(), P()),
        check_vma=False,
    )
```

profile of v0, /device:TPU:0, one launch (start us, length us, event | category | flops | bytes accessed | tf_op | source)
XLA Modules:
  0.0 268.8 jit_solution(7776146395088304549)
XLA Ops:
  8.1 1.2 copy-done
  9.2 11.5 %convolution_convert_fusion = bf16[256,4096]{1,0:T(8,128)(2,1)} fusion(bf16[256,2048]{1,0:T(8,128)(2,1)S(1)} %copy-done, bf16[2048,4096]{1,0:T(8,128)(2,1)} %param.15), kind=kOutput, calls=%fused_computation.1 | convolution fusion | flops 4296015872 | bytes 19922944 | tf_op jit(solution)/shard_map/dot_general | solution.py:42
  20.7 0.0 all-gather.2.cloned.1.call-start
  20.8 0.5 all-gather.2.cloned.1.call-update
  21.3 0.0 reduce-scatter.7.cloned.1.call-start
  21.4 0.6 fusion.13
  22.0 0.1 select_reduce_fusion
  22.1 33.5 %reduce-scatter.5.cloned.1.call-done = bf16[128,4096]{1,0:T(8,128)(2,1)} async-done(((bf16[256,4096]{1,0:T(8,128)(2,1)}), bf16[128,4096]{1,0:T(8,128)(2,1)}) %reduce-scatter.5.cloned.1.call-update) | async-done | bytes 1048592 | tf_op jit(solution)/shard_map/reduce_scatter | solution.py:41
  55.7 1.7 fusion.3
  57.3 0.5 multiply_reduce_fusion
  57.9 2.2 fusion.15
  60.1 46.4 %all-gather.2.cloned.1.call-done = bf16[3072,768]{1,0:T(8,128)(2,1)} async-done(((bf16[96,768]{1,0:T(8,128)(2,1)}), bf16[3072,768]{1,0:T(8,128)(2,1)}) %all-gather.2.cloned.1.call-update) | async-done | bytes 4718608 | tf_op jit(solution)/shard_map/all_gather | solution.py:54
  106.5 3.2 %fusion.14 = (f32[128]{0:T(128)S(1)}, f32[128,768]{1,0:T(8,128)S(1)}) fusion(bf16[128,3072]{1,0:T(8,128)(2,1)S(1)} %copy-done.3, bf16[3072,768]{1,0:T(8,128)(2,1)} %all-gather.2.cloned.1.call-done, bf16[128,768]{1,0:T(8,128)(2,1)S(1)} %copy-done.4), kind=kOutput, calls=%fused_computation.48 | convolution fusion | flops 604274560 | bytes 6095360 | tf_op jit(solution)/shard_map/dot_general | solution.py:21
  109.8 0.2 multiply_reduce_fusion.2
  110.0 0.1 multiply_convert_fusion.1
  110.1 0.1 fusion.16
  110.2 0.1 exponential_reduce_fusion.1
  110.4 0.6 convert_reduce_fusion
  111.0 0.4 fusion.11
  111.4 5.2 %convolution_bitcast_fusion = f32[3072,768]{0,1:T(8,128)} fusion(bf16[128,3072]{1,0:T(8,128)(2,1)S(1)} %copy-done.3, f32[128,768]{1,0:T(8,128)S(1)} %get-tuple-element.31, f32[128,768]{1,0:T(8,128)S(1)} %get-tuple-element.26, f32[128]{0:T(128)S(1)} %get-tuple-element.32, f32[128]{0:T(128)S(1)} %get-tuple-element.33, f32[128]{0:T(128)S(1)} %add_rsqrt_fusion.1, ...), kind=kOutput, calls=%fused_computation | convolution fusion | flops 604667904 | bytes 11012096 | tf_op jit(solution)/shard_map/dot_general | solution.py:96
  116.6 9.6 %copy.19 = f32[3072,768]{1,0:T(8,128)} copy(f32[3072,768]{0,1:T(8,128)} %convolution_bitcast_fusion) | data formatting | bytes 18874368
  126.3 0.1 fusion.17
  126.4 39.3 %all-reduce = (f32[768,4]{0,1:T(4,128)}, f32[]{:T(128)}, f32[]{:T(128)}) all-reduce(f32[768,4]{0,1:T(4,128)S(1)} %fusion.17, f32[]{:T(128)} %get-tuple-element.18, f32[]{:T(128)} %get-tuple-element.17), channel_id=1, replica_groups=mesh['dp'=16,'tensor'=2] {'dp','tensor'}, use_global_device_ids=true, to_apply=%region_11.13 | all-reduce | flops 3074 | bytes 24592 | tf_op jit(solution)/shard_map/psum | solution.py:103
  167.0 93.2 %reduce-scatter.7.cloned.1.call-done = f32[96,768]{1,0:T(8,128)} async-done(((f32[3072,768]{1,0:T(8,128)}), f32[96,768]{1,0:T(8,128)}) %reduce-scatter.7.cloned.1.call-update) | async-done | bytes 294928
  (39 shorter events, 0.3 us)
Async XLA Ops:
  8.0 1.2 copy-start
  8.0 47.6 %reduce-scatter.5.cloned.1.call-start = ((), (), s32[]{:S(2)}) async-start(), calls=%async_computation.3 | async-start | bytes 3145728 | tf_op jit(solution)/shard_map/reduce_scatter | solution.py:41
  20.7 0.7 copy-start.8
  20.7 0.7 copy-start.6
  20.7 0.8 copy-start.9
  20.7 1.3 copy-start.11
  20.7 35.0 %copy-start.1 = (bf16[128,4096]{1,0:T(8,128)(2,1)S(1)}, bf16[128,4096]{1,0:T(8,128)(2,1)}, u32[]{:S(2)}) copy-start(bf16[128,4096]{1,0:T(8,128)(2,1)} %param.16) | copy-start | bytes 3145732
  20.7 85.8 %all-gather.2.cloned.1.call-start = ((), (), s32[]{:S(2)}) async-start(), calls=%async_computation.2 | async-start | bytes 4866048 | tf_op jit(solution)/shard_map/all_gather | solution.py:54
  21.3 238.9 %reduce-scatter.7.cloned.1.call-start = ((), (), s32[]{:S(2)}) async-start(), calls=%async_computation.4 | async-start | bytes 9732096
  22.1 35.8 %copy-start.10 = (bf16[4096,4]{0,1:T(4,128)(2,1)S(1)}, bf16[4096,4]{0,1:T(4,128)(2,1)}, u32[]{:S(2)}) copy-start(bf16[4096,4]{0,1:T(4,128)(2,1)} %param.19) | copy-start | bytes 98308
  55.7 1.7 copy-start.2
  57.9 48.6 %copy-start.3 = (bf16[128,3072]{1,0:T(8,128)(2,1)S(1)}, bf16[128,3072]{1,0:T(8,128)(2,1)}, u32[]{:S(2)}) copy-start(bf16[128,3072]{1,0:T(8,128)(2,1)} %param.20) | copy-start | bytes 2359300
  57.9 48.6 %copy-start.4 = (bf16[128,768]{1,0:T(8,128)(2,1)S(1)}, bf16[128,768]{1,0:T(8,128)(2,1)}, u32[]{:S(2)}) copy-start(bf16[128,768]{1,0:T(8,128)(2,1)} %param.21) | copy-start | bytes 589828
  60.1 50.0 %copy-start.5 = (bf16[768,4]{0,1:T(4,128)(2,1)S(1)}, bf16[768,4]{0,1:T(4,128)(2,1)}, u32[]{:S(2)}) copy-start(bf16[768,4]{0,1:T(4,128)(2,1)} %param.24) | copy-start | bytes 18436
  60.1 50.2 %copy-start.7 = (s32[128]{0:T(128)S(1)}, s32[128]{0:T(128)}, u32[]{:S(2)}) copy-start(s32[128]{0:T(128)} %param.25) | copy-start | bytes 1540
Sparse Core Ops, SparseCore 0:
  20.9 34.7 reduce-scatter.4
Sparse Core Ops, SparseCore 1:
  24.1 82.3 all-gather.1
  126.4 133.8 reduce-scatter.6
where the time goes:
time: 269 us
  waiting for transfers between devices  174 us (65%)
  blocking collectives  39.3 us (15%)
  matrix products  22.7 us (8%)
  between operations  18.1 us (7%)
  local copies, waits for them, and re-layouts  11.5 us (4%)
  other arithmetic  3.44 us (1%)
    unnamed x4, waiting for transfers between devices  93.8 us
    all_gather x1, waiting for transfers between devices, local(): lax.all_gather(down_weight, ('dp', 'tensor'), axis=0, tiled=True)  46.4 us
    psum x1, blocking collectives, local(): lax.psum((head_term, loss_part, jnp.sum(validity)), ('dp', 'tensor'))  39.3 us
    reduce_scatter x1, waiting for transfers between devices, local(): lax.psum_scatter(jnp.dot(context, w_out, preferred_element_type=jnp.float...  33.5 us
    dot_general x1, matrix products, local(): jnp.dot(context, w_out, preferred_element_type=jnp.float32)  11.5 us
    unnamed x25, local copies, waits for them, and re-layouts  10.9 us
  transfers between devices with their start and end apart: 3, of which 3 were waited for; matrix products, arithmetic and copies ran while one was open for 2% of the time, Pallas kernels for 0%

commit v1 on v0

--- a/solution.py
+++ b/solution.py
@@ -101,7 +101,7 @@
         tiled=True,
     )
     head_total, loss_total, count_total = lax.psum(
-        (head_term, loss_part, jnp.sum(validity)), ("dp", "tensor")
+        lax.psum((head_term, loss_part, jnp.sum(validity)), "tensor"), "dp"
     )
     return (grad_down, head_total, loss_total / count_total)
 

time: 269 us -> 269 us (level)
  waiting for transfers between devices: 174 us -> 145 us
  blocking collectives: 39.3 us -> 67.9 us
    unnamed x4, waiting for transfers between devices: 93.8 us -> 65.1 us
    psum x1 -> x2, blocking collectives: 39.3 us -> 67.9 us  [the longest x1 58.6 us: local(): lax.psum(lax.psum((head_term, loss_part, jnp.sum(validity)), 'tensor'), '...]
where the time goes in v1:
time: 269 us
  waiting for transfers between devices  145 us (54%)
  blocking collectives  67.9 us (25%)
  matrix products  22.7 us (8%)
  between operations  18.2 us (7%)
  local copies, waits for them, and re-layouts  11.5 us (4%)
  other arithmetic  3.41 us (1%)
    unnamed x4, waiting for transfers between devices  65.1 us
    psum x1, blocking collectives, local(): lax.psum(lax.psum((head_term, loss_part, jnp.sum(validity)), 'tensor'), '...  58.6 us
    all_gather x1, waiting for transfers between devices, local(): lax.all_gather(down_weight, ('dp', 'tensor'), axis=0, tiled=True)  46.4 us
    reduce_scatter x1, waiting for transfers between devices, local(): lax.psum_scatter(jnp.dot(context, w_out, preferred_element_type=jnp.float...  33.5 us
    dot_general x1, matrix products, local(): jnp.dot(context, w_out, preferred_element_type=jnp.float32)  11.5 us
    unnamed x25, local copies, waits for them, and re-layouts  10.9 us
    psum x1, blocking collectives, local(): lax.psum((head_term, loss_part, jnp.sum(validity)), 'tensor')  9.31 us
  transfers between devices with their start and end apart: 3, of which 3 were waited for; matrix products, arithmetic and copies ran while one was open for 2% of the time, Pallas kernels for 0%

profile of v1, /device:TPU:0, one launch (start us, length us, event | category | flops | bytes accessed | tf_op | source)
XLA Modules:
  0.0 268.8 jit_solution(11434386944062099820)
XLA Ops:
  8.1 1.2 copy-done
  9.2 11.5 %convolution_convert_fusion = bf16[256,4096]{1,0:T(8,128)(2,1)} fusion(bf16[256,2048]{1,0:T(8,128)(2,1)S(1)} %copy-done, bf16[2048,4096]{1,0:T(8,128)(2,1)} %param.15), kind=kOutput, calls=%fused_computation.1 | convolution fusion | flops 4296015872 | bytes 19922944 | tf_op jit(solution)/shard_map/dot_general | solution.py:42
  20.7 0.0 all-gather.2.cloned.1.call-start
  20.8 0.5 all-gather.2.cloned.1.call-update
  21.4 0.6 fusion.13
  22.0 0.1 select_reduce_fusion
  22.1 33.5 %reduce-scatter.5.cloned.1.call-done = bf16[128,4096]{1,0:T(8,128)(2,1)} async-done(((bf16[256,4096]{1,0:T(8,128)(2,1)}), bf16[128,4096]{1,0:T(8,128)(2,1)}) %reduce-scatter.5.cloned.1.call-update) | async-done | bytes 1048592 | tf_op jit(solution)/shard_map/reduce_scatter | solution.py:41
  55.7 1.7 fusion.3
  57.3 0.5 multiply_reduce_fusion
  57.9 2.2 fusion.15
  60.1 46.4 %all-gather.2.cloned.1.call-done = bf16[3072,768]{1,0:T(8,128)(2,1)} async-done(((bf16[96,768]{1,0:T(8,128)(2,1)}), bf16[3072,768]{1,0:T(8,128)(2,1)}) %all-gather.2.cloned.1.call-update) | async-done | bytes 4718608 | tf_op jit(solution)/shard_map/all_gather | solution.py:54
  106.5 3.2 %fusion.14 = (f32[128]{0:T(128)S(1)}, f32[128,768]{1,0:T(8,128)S(1)}) fusion(bf16[128,3072]{1,0:T(8,128)(2,1)S(1)} %copy-done.3, bf16[3072,768]{1,0:T(8,128)(2,1)} %all-gather.2.cloned.1.call-done, bf16[128,768]{1,0:T(8,128)(2,1)S(1)} %copy-done.4), kind=kOutput, calls=%fused_computation.48 | convolution fusion | flops 604274560 | bytes 6095360 | tf_op jit(solution)/shard_map/dot_general | solution.py:21
  109.8 0.2 multiply_reduce_fusion.2
  110.0 0.1 multiply_convert_fusion.1
  110.1 0.1 fusion.16
  110.2 0.1 exponential_reduce_fusion.1
  110.4 0.6 convert_reduce_fusion
  111.0 0.4 fusion.11
  111.4 5.2 %convolution_bitcast_fusion = f32[3072,768]{0,1:T(8,128)} fusion(bf16[128,3072]{1,0:T(8,128)(2,1)S(1)} %copy-done.3, f32[128,768]{1,0:T(8,128)S(1)} %get-tuple-element.34, f32[128,768]{1,0:T(8,128)S(1)} %get-tuple-element.29, f32[128]{0:T(128)S(1)} %get-tuple-element.35, f32[128]{0:T(128)S(1)} %get-tuple-element.36, f32[128]{0:T(128)S(1)} %add_rsqrt_fusion.1, ...), kind=kOutput, calls=%fused_computation | convolution fusion | flops 604667904 | bytes 11012096 | tf_op jit(solution)/shard_map/dot_general | solution.py:96
  116.6 9.6 %copy.19 = f32[3072,768]{1,0:T(8,128)} copy(f32[3072,768]{0,1:T(8,128)} %convolution_bitcast_fusion) | data formatting | bytes 18874368
  126.2 0.1 fusion.17
  126.4 9.3 %all-reduce.1 = (f32[768,4]{0,1:T(4,128)S(1)}, f32[]{:T(128)}, f32[]{:T(128)}) all-reduce(f32[768,4]{0,1:T(4,128)S(1)} %fusion.17, f32[]{:T(128)} %get-tuple-element.18, f32[]{:T(128)} %get-tuple-element.17), channel_id=1, replica_groups=mesh['dp'=16,'tensor'=2] {'tensor'}, use_global_device_ids=true, to_apply=%region_11.13 | all-reduce | flops 3074 | bytes 24592 | tf_op jit(solution)/shard_map/psum | solution.py:104
  135.7 58.6 %all-reduce = (f32[768,4]{0,1:T(4,128)}, f32[]{:T(128)}, f32[]{:T(128)}) all-reduce(f32[768,4]{0,1:T(4,128)S(1)} %get-tuple-element.22, f32[]{:T(128)} %get-tuple-element.23, f32[]{:T(128)} %get-tuple-element.24), channel_id=1, replica_groups=mesh['dp'=16,'tensor'=2] {'dp'}, use_global_device_ids=true, to_apply=%region_12.14 | all-reduce | flops 3074 | bytes 24592 | tf_op jit(solution)/shard_map/psum | solution.py:103
  195.7 64.6 %reduce-scatter.7.cloned.1.call-done = f32[96,768]{1,0:T(8,128)} async-done(((f32[3072,768]{1,0:T(8,128)}), f32[96,768]{1,0:T(8,128)}) %reduce-scatter.7.cloned.1.call-update) | async-done | bytes 294928
  (40 shorter events, 0.3 us)
Async XLA Ops:
  8.0 1.2 copy-start
  8.0 47.6 %reduce-scatter.5.cloned.1.call-start = ((), (), s32[]{:S(2)}) async-start(), calls=%async_computation.3 | async-start | bytes 3145728 | tf_op jit(solution)/shard_map/reduce_scatter | solution.py:41
  20.7 0.7 copy-start.8
  20.7 0.7 copy-start.6
  20.7 0.8 copy-start.9
  20.7 1.3 copy-start.11
  20.7 35.0 %copy-start.1 = (bf16[128,4096]{1,0:T(8,128)(2,1)S(1)}, bf16[128,4096]{1,0:T(8,128)(2,1)}, u32[]{:S(2)}) copy-start(bf16[128,4096]{1,0:T(8,128)(2,1)} %param.16) | copy-start | bytes 3145732
  20.7 85.8 %all-gather.2.cloned.1.call-start = ((), (), s32[]{:S(2)}) async-start(), calls=%async_computation.2 | async-start | bytes 4866048 | tf_op jit(solution)/shard_map/all_gather | solution.py:54
  21.3 238.9 %reduce-scatter.7.cloned.1.call-start = ((), (), s32[]{:S(2)}) async-start(), calls=%async_computation.4 | async-start | bytes 9732096
  22.1 35.8 %copy-start.10 = (bf16[4096,4]{0,1:T(4,128)(2,1)S(1)}, bf16[4096,4]{0,1:T(4,128)(2,1)}, u32[]{:S(2)}) copy-start(bf16[4096,4]{0,1:T(4,128)(2,1)} %param.19) | copy-start | bytes 98308
  55.7 1.7 copy-start.2
  57.9 48.6 %copy-start.3 = (bf16[128,3072]{1,0:T(8,128)(2,1)S(1)}, bf16[128,3072]{1,0:T(8,128)(2,1)}, u32[]{:S(2)}) copy-start(bf16[128,3072]{1,0:T(8,128)(2,1)} %param.20) | copy-start | bytes 2359300
  57.9 48.6 %copy-start.4 = (bf16[128,768]{1,0:T(8,128)(2,1)S(1)}, bf16[128,768]{1,0:T(8,128)(2,1)}, u32[]{:S(2)}) copy-start(bf16[128,768]{1,0:T(8,128)(2,1)} %param.21) | copy-start | bytes 589828
  60.1 50.0 %copy-start.5 = (bf16[768,4]{0,1:T(4,128)(2,1)S(1)}, bf16[768,4]{0,1:T(4,128)(2,1)}, u32[]{:S(2)}) copy-start(bf16[768,4]{0,1:T(4,128)(2,1)} %param.24) | copy-start | bytes 18436
  60.1 50.2 %copy-start.7 = (s32[128]{0:T(128)S(1)}, s32[128]{0:T(128)}, u32[]{:S(2)}) copy-start(s32[128]{0:T(128)} %param.25) | copy-start | bytes 1540
Sparse Core Ops, SparseCore 0:
  20.9 34.7 reduce-scatter.4
Sparse Core Ops, SparseCore 1:
  24.1 82.3 all-gather.1
  126.3 133.9 reduce-scatter.6
